TPU v7x, 128 devices: a whole 4x4x4 slice. The times are simulated.
128 devices in a mesh: group: 4 (over x), expert: 32 (over y, z, core).
Axes of the slice: x: 4, y: 4, z: 4, core: 2. Of those that a mesh axis runs over, the one named last changes fastest.
Arguments:
- tokens: bfloat16 [16384, 2048], P(('group', 'expert')), may hold values from -6 to 6
- cotangent: bfloat16 [16384, 2048], P(('group', 'expert')), may hold values from -6 to 6
- gate_probs: float32 [16384, 8], P(('group', 'expert')), may hold values from 0.02 to 0.5
- expert_ids: int32 [16384, 8], P(('group', 'expert')), may hold values from 0 to 31, all different within a row; in each aligned block of 128 rows (0 to 127, 128 to 255, ...) at most 72 rows name the same one
- gate_up: bfloat16 [32, 2048, 768], P('expert'), may hold values from -0.125 to 0.125
- down_weight: bfloat16 [32, 384, 2048], P('expert'), may hold values from -0.3125 to 0.3125
- gate_up_moment: float32 [32, 2048, 768], P('expert', 'group'), may hold values from -6 to 6
- gate_up_second: float32 [32, 2048, 768], P('expert', 'group'), may hold values from 0.05 to 20
- down_moment: float32 [32, 384, 2048], P('expert', None, 'group'), may hold values from -6 to 6
- down_second: float32 [32, 384, 2048], P('expert', None, 'group'), may hold values from 0.05 to 20
Outputs:
- token_grad: bfloat16 [16384, 2048], P(('group', 'expert'))
- updated_gate_up: bfloat16 [32, 2048, 768], P('expert')
- updated_down: bfloat16 [32, 384, 2048], P('expert')
- gate_up_moment_out: float32 [32, 2048, 768], P('expert', 'group')
- gate_up_second_out: float32 [32, 2048, 768], P('expert', 'group')
- down_moment_out: float32 [32, 384, 2048], P('expert', None, 'group')
- down_second_out: float32 [32, 384, 2048], P('expert', None, 'group')
Inputs may be any that keep to these rules, and one draw needn't show every extreme that they name: `expert_ids`: each row names 8 different experts. In the rows of one device no expert is named by more than 72 rows, and in every draw some expert is named by exactly 72 rows of some device.
All inputs are finite; a program needn't handle non-finite values.
Results may differ from a plain program's by a relative error of at most 0.015.
Values may be sent and summed in bfloat16 or wider, within the bound.
No kernel may reach another device: no remote copies, remote signals or barrier semaphores. Data moves between devices by JAX's collectives and lax.ppermute only.
A program may use at most 192 MiB of HBM per device.

v0:
```python
import jax
import jax.numpy as jnp
from jax import lax
from jax.sharding import PartitionSpec as P

learn_rate = 0.001
beta_first = 0.9
beta_second = 0.999
adam_eps = 1e-08


def expert_backward(inputs, scaled_parts, weight_gate_up, weight_down):
    hidden_count = weight_down.shape[0]
    width = scaled_parts[0].shape[1]
    projected = jnp.dot(inputs, weight_gate_up, preferred_element_type=jnp.float32)
    gate_part = projected[:, :hidden_count]
    up_part = projected[:, hidden_count:]
    sigmoid_gate = jax.nn.sigmoid(gate_part)
    activated = gate_part * sigmoid_gate
    hidden_act = (activated * up_part).astype(jnp.bfloat16)
    hidden_grad = sum(
        (
            jnp.dot(
                part,
                weight_down[:, i * width : (i + 1) * width].T,
                preferred_element_type=jnp.float32,
            )
            for i, part in enumerate(scaled_parts)
        )
    )
    slope = sigmoid_gate * (1.0 + gate_part * (1.0 - sigmoid_gate))
    hidden_act, up_slope, activated = lax.optimization_barrier(
        (hidden_act, up_part * slope, activated)
    )
    pair_grad = jnp.concatenate([hidden_grad * up_slope, hidden_grad * activated], axis=1).astype(
        jnp.bfloat16
    )
    down_grad = jnp.dot(
        hidden_act.T, jnp.concatenate(scaled_parts, axis=1), preferred_element_type=jnp.float32
    )
    gate_up_grad = jnp.dot(inputs.T, pair_grad, preferred_element_type=jnp.float32)
    input_grad = jnp.dot(pair_grad, weight_gate_up.T, preferred_element_type=jnp.float32).astype(
        jnp.bfloat16
    )
    return (gate_up_grad, down_grad, input_grad)


def adam_update(weight, grad, first, second):
    first_new = beta_first * first + (1.0 - beta_first) * grad
    second_new = beta_second * second + (1.0 - beta_second) * grad * grad
    updated = (
        weight.astype(jnp.float32) - learn_rate * first_new / (jnp.sqrt(second_new) + adam_eps)
    ).astype(jnp.bfloat16)
    return (updated, first_new, second_new)


def exclusive_count(flags):
    n = flags.shape[-1]
    earlier = (jnp.arange(n)[:, None] < jnp.arange(n)[None, :]).astype(jnp.bfloat16)
    return jnp.dot(flags.astype(jnp.bfloat16), earlier, preferred_element_type=jnp.float32)


def local(
    tokens,
    cotangent,
    gate_probs,
    expert_ids,
    gate_up,
    down_weight,
    gate_up_moment,
    gate_up_second,
    down_moment,
    down_second,
):
    expert_count = lax.axis_size("expert")
    me = lax.axis_index("expert")
    local_tokens, model_width = tokens.shape
    top_count = expert_ids.shape[1]
    capacity = min(local_tokens, 9 * local_tokens * top_count // (4 * expert_count))
    slot_total = expert_count * capacity
    half_width = model_width // 2
    pieces = []
    rest = gate_probs
    for _ in range(3):
        piece = lax.reduce_precision(rest, exponent_bits=8, mantissa_bits=7)
        pieces.append(piece)
        rest = rest - piece
    meta = jnp.concatenate([expert_ids.astype(jnp.float32)] + pieces, axis=1)
    meta_width = 128
    meta = jnp.pad(meta, ((0, 0), (0, meta_width - meta.shape[1]))).astype(jnp.bfloat16)
    first = lax.all_gather(
        jnp.concatenate([tokens, cotangent[:, :half_width], meta], axis=1), "expert", axis=0
    )
    first, cot_after = lax.optimization_barrier((first, cotangent))
    cot_hi = lax.all_gather(cot_after[:, half_width:], "expert", axis=0)
    meta_at = model_width + half_width
    all_meta = first[..., meta_at : meta_at + 4 * top_count].astype(jnp.float32)
    all_ids = all_meta[..., :top_count].astype(jnp.int32)
    all_gates = (
        all_meta[..., top_count : 2 * top_count]
        + all_meta[..., 2 * top_count : 3 * top_count]
        + all_meta[..., 3 * top_count :]
    )
    match = all_ids == me
    routed = jnp.any(match, axis=-1).astype(jnp.float32)
    gate_of = jnp.sum(jnp.where(match, all_gates, 0.0), axis=-1)
    rank = exclusive_count(routed)
    slots = jnp.arange(capacity, dtype=jnp.float32)
    pick = (routed[:, None, :] > 0) & (rank[:, None, :] == slots[None, :, None])
    pick_b = pick.astype(jnp.bfloat16)
    picked_first = jnp.einsum(
        "srt,stc->src", pick_b, first, preferred_element_type=jnp.float32
    ).astype(jnp.bfloat16)
    inputs = picked_first[..., :model_width]
    slot_gate = jnp.sum(jnp.where(pick, gate_of[:, None, :], 0.0), axis=-1)
    picked_hi = jnp.einsum(
        "srt,stc->src", pick_b, cot_hi, preferred_element_type=jnp.float32
    ).astype(jnp.bfloat16)
    scaled = [
        (slot_gate[..., None] * part.astype(jnp.float32))
        .astype(jnp.bfloat16)
        .reshape(slot_total, half_width)
        for part in (picked_first[..., model_width:meta_at], picked_hi)
    ]
    weight_pair = gate_up[0]
    weight_down = down_weight[0]
    grad_pair, grad_down, row_grads = expert_backward(
        inputs.reshape(slot_total, model_width), scaled, weight_pair, weight_down
    )
    dense = jnp.einsum(
        "srt,src->stc",
        pick_b,
        row_grads.reshape(expert_count, capacity, model_width),
        preferred_element_type=jnp.float32,
    ).astype(jnp.bfloat16)
    token_grad = lax.psum_scatter(
        dense.reshape(expert_count * local_tokens, model_width),
        "expert",
        scatter_dimension=0,
        tiled=True,
    )
    groups = lax.axis_size("group")
    share_rows = model_width // groups
    hidden_count = grad_down.shape[0]
    pair_width = grad_pair.shape[1]
    pair_parts = lax.all_to_all(
        grad_pair.astype(jnp.bfloat16).reshape(groups, share_rows, pair_width),
        "group",
        0,
        0,
        tiled=True,
    )
    down_parts = lax.all_to_all(
        grad_down.astype(jnp.bfloat16).reshape(hidden_count, groups, share_rows),
        "group",
        1,
        1,
        tiled=True,
    )
    sum_pair = jnp.sum(pair_parts.astype(jnp.float32), axis=0)[None]
    sum_down = jnp.sum(down_parts.astype(jnp.float32), axis=1)[None]
    token_grad, sum_down = lax.optimization_barrier((token_grad, sum_down))
    group_index = lax.axis_index("group")
    own_pair = lax.dynamic_slice_in_dim(gate_up, group_index * share_rows, share_rows, 1)
    own_down = lax.dynamic_slice_in_dim(down_weight, group_index * share_rows, share_rows, 2)
    new_pair, first_pair, second_pair = adam_update(
        own_pair, sum_pair, gate_up_moment, gate_up_second
    )
    new_down, first_down, second_down = adam_update(own_down, sum_down, down_moment, down_second)
    full_pair = lax.all_to_all(
        jnp.broadcast_to(new_pair, (groups, share_rows, pair_width)), "group", 0, 0, tiled=True
    ).reshape(1, model_width, pair_width)
    full_down = lax.all_gather(new_down, "group", axis=2, tiled=True)
    return (token_grad, full_pair, full_down, first_pair, second_pair, first_down, second_down)


def solution(mesh):
    rows = P(("group", "expert"), None)
    placed = (
        rows,
        rows,
        rows,
        rows,
        P("expert", None, None),
        P("expert", None, None),
        P("expert", "group", None),
        P("expert", "group", None),
        P("expert", None, "group"),
        P("expert", None, "group"),
    )
    return jax.shard_map(
        local,
        mesh=mesh,
        in_specs=placed,
        out_specs=(
            rows,
            P("expert", None, None),
            P("expert", None, None),
            P("expert", "group", None),
            P("expert", "group", None),
            P("expert", None, "group"),
            P("expert", None, "group"),
        ),
        check_vma=False,
    )
```

profile of v0, /device:TPU:1, one launch (start us, length us, event | category | flops | bytes accessed | tf_op | source)
XLA Modules:
  0.0 347.5 jit_solution(9185191989546034513)
XLA Ops:
  11.8 98.6 %all-gather.8.cloned.1.call-done = bf16[4096,3200]{1,0:T(8,128)(2,1)} async-done(((bf16[128,3200]{1,0:T(8,128)(2,1)}), bf16[4096,3200]{1,0:T(8,128)(2,1)}) %all-gather.8.cloned.1.call-update) | async-done | bytes 26214416 | tf_op jit(solution)/shard_map/all_gather | solution.py:91
  112.7 3.0 fusion.12
  116.9 15.9 %convolution_convert_fusion.1 = bf16[32,72,3200]{2,1,0:T(8,128)(2,1)} fusion(bf16[32,128,3200]{2,1,0:T(8,128)(2,1)} %bitcast.41, f32[32,128]{1,0:T(8,128)S(1)} %fusion.33, pred[32,128]{1,0:T(8,128)(4,1)S(1)} %convert_compare_fusion), kind=kOutput, calls=%fused_computation.1 | convolution fusion | flops 1895399424 | bytes 40980480 | tf_op jit(solution)/shard_map/srt,stc->src/dot_general | solution.py:111
  132.8 9.4 %slice.59 = bf16[32,72,2048]{2,1,0:T(8,128)(2,1)} slice(bf16[32,72,3200]{2,1,0:T(8,128)(2,1)} %convolution_convert_fusion.1), slice={[0:32], [0:72], [0:2048]} | slice | bytes 18874368 | tf_op jit(solution)/shard_map/slice | solution.py:114
  142.3 10.6 %fusion.6 = f32[2304,768]{0,1:T(8,128)S(1)} fusion(bf16[2304,2048]{1,0:T(8,128)(2,1)} %bitcast.44, bf16[1,2048,768]{2,1,0:T(8,128)(2,1)S(1)} %copy-done.15), kind=kOutput, calls=%fused_computation.20 | convolution fusion | flops 7247757312 | bytes 19660800 | tf_op jit(solution)/shard_map/dot_general | solution.py:15
  152.9 3.2 fusion.4
  156.8 3.5 %multiply_convert_fusion.1 = bf16[32,72,1024]{2,1,0:T(8,128)(2,1)S(1)} fusion(bf16[32,72,3200]{2,1,0:T(8,128)(2,1)} %convolution_convert_fusion.1, f32[32,72]{1,0:T(8,128)S(1)} %select_reduce_fusion), kind=kLoop, calls=%fused_computation.8 | loop fusion | flops 7077888 | bytes 9446400 | tf_op jit(solution)/shard_map/convert_element_type | solution.py:121
  162.5 3.8 %fusion.24 = f32[2304,384]{0,1:T(8,128)} fusion(bf16[2304,1024]{1,0:T(8,128)(2,1)S(1)} %bitcast.47, bf16[384,2048]{1,0:T(8,128)(2,1)S(1)} %bitcast.52), kind=kOutput, calls=%fused_computation.46 | convolution fusion | flops 1811939328 | bytes 9043968 | tf_op jit(solution)/shard_map/dot_general | solution.py:23
  166.3 4.9 %multiply_convert_fusion = bf16[32,72,1024]{2,1,0:T(8,128)(2,1)S(1)} fusion(f32[32,72]{1,0:T(8,128)} %copy-done.16, bf16[32,128,1024]{2,1,0:T(8,128)(2,1)} %bitcast.46, f32[32,128]{1,0:T(8,128)S(1)} %fusion.33, pred[32,128]{1,0:T(8,128)(4,1)} %copy-done.17), kind=kOutput, calls=%fused_computation.7 | convolution fusion | flops 614006784 | bytes 13136896 | tf_op jit(solution)/shard_map/srt,stc->src/dot_general | solution.py:116
  174.7 11.2 %convolution_convert_fusion.2 = bf16[2304,2048]{1,0:T(8,128)(2,1)S(1)} fusion(bf16[1,2048,768]{2,1,0:T(8,128)(2,1)} %param.14, bf16[2304,384]{0,1:T(8,128)(2,1)S(1)} %get-tuple-element.33, bf16[2304,384]{0,1:T(8,128)(2,1)S(1)} %get-tuple-element.32), kind=kOutput, calls=%fused_computation.2 | convolution fusion | flops 7259553792 | bytes 16121856 | tf_op jit(solution)/shard_map/dot_general | solution.py:42
  185.9 8.2 %convolution_convert_fusion = bf16[32,128,2048]{2,1,0:T(8,128)(2,1)} fusion(bf16[32,72,2048]{2,1,0:T(8,128)(2,1)S(1)} %bitcast.42, f32[32,128]{1,0:T(8,128)S(1)} %fusion.33, pred[32,128]{1,0:T(8,128)(4,1)S(1)} %copy-done.19), kind=kOutput, calls=%fused_computation | convolution fusion | flops 1216937984 | bytes 26234880 | tf_op jit(solution)/shard_map/srt,src->stc/dot_general | solution.py:130
  195.6 7.6 %fusion.8 = bf16[384,2048]{1,0:T(8,128)(2,1)S(1)} fusion(bf16[2304,384]{0,1:T(8,128)(2,1)S(1)} %copy-done.8, bf16[2304,1024]{1,0:T(8,128)(2,1)} %bitcast.39, bf16[2304,1024]{1,0:T(8,128)(2,1)} %bitcast.48), kind=kOutput, calls=%fused_computation.23 | convolution fusion | flops 3643539456 | bytes 12779520 | tf_op jit(solution)/shard_map/dot_general | solution.py:38
  204.5 3.8 %all-to-all-start = ((bf16[384,4,512]{2,0,1:T(8,128)(2,1)}), bf16[384,4,512]{2,0,1:T(8,128)(2,1)S(1)}, u32[]{:S(2)}, u32[]{:S(2)}) async-start(bf16[384,4,512]{2,0,1:T(8,128)(2,1)} %bitcast.36), calls=%async_computation.1 | async-start | bytes 3145728 | tf_op jit(solution)/shard_map/all_to_all | solution.py:153
  208.3 12.5 %convolution_convert_fusion.3 = bf16[2048,768]{1,0:T(8,128)(2,1)} fusion(bf16[2304,2048]{1,0:T(8,128)(2,1)} %bitcast.45, bf16[2304,384]{0,1:T(8,128)(2,1)} %copy-done.6, bf16[2304,384]{0,1:T(8,128)(2,1)S(1)} %copy-done.5), kind=kOutput, calls=%fused_computation.18 | convolution fusion | flops 7256408064 | bytes 16121856 | tf_op jit(solution)/shard_map/dot_general | solution.py:41
  220.8 7.9 %all-to-all-done = bf16[384,4,512]{2,0,1:T(8,128)(2,1)S(1)} async-done(((bf16[384,4,512]{2,0,1:T(8,128)(2,1)}), bf16[384,4,512]{2,0,1:T(8,128)(2,1)S(1)}, u32[]{:S(2)}, u32[]{:S(2)}) %all-to-all-start) | async-done | bytes 1572896 | tf_op jit(solution)/shard_map/all_to_all | solution.py:153
  229.8 3.8 %all-to-all-start.1 = ((bf16[4,512,768]{2,1,0:T(8,128)(2,1)}), bf16[4,512,768]{2,1,0:T(8,128)(2,1)S(1)}, u32[]{:S(2)}, u32[]{:S(2)}) async-start(bf16[4,512,768]{2,1,0:T(8,128)(2,1)} %bitcast.49), calls=%async_computation.2 | async-start | bytes 6291456 | tf_op jit(solution)/shard_map/all_to_all | solution.py:146
  233.7 2.7 convert_reduce_fusion.1
  236.4 33.5 %all-to-all-done.1 = bf16[4,512,768]{2,1,0:T(8,128)(2,1)S(1)} async-done(((bf16[4,512,768]{2,1,0:T(8,128)(2,1)}), bf16[4,512,768]{2,1,0:T(8,128)(2,1)S(1)}, u32[]{:S(2)}, u32[]{:S(2)}) %all-to-all-start.1) | async-done | bytes 3145760 | tf_op jit(solution)/shard_map/all_to_all | solution.py:146
  271.9 3.9 %fusion.26 = (bf16[512,768]{1,0:T(8,128)(2,1)S(1)}, f32[1,512,768]{2,1,0:T(8,128)}, f32[1,512,768]{2,1,0:T(8,128)}) fusion(bf16[1,2048,768]{2,1,0:T(8,128)(2,1)} %param.14, s32[]{:T(128)S(6)} %select_n.14, f32[512,768]{1,0:T(8,128)S(1)} %convert_reduce_fusion, f32[1,512,768]{2,1,0:T(8,128)S(1)} %copy-done.9, f32[1,512,768]{2,1,0:T(8,128)S(1)} %copy-done.10), kind=kLoop, calls=%fused_computation.50 | loop fusion | flops 5111808 | bytes 9437188 | tf_op jit(solution)/shard_map/broadcast_in_dim | solution.py:171
  277.6 3.7 %all-to-all-start.2 = ((bf16[4,512,768]{2,1,0:T(8,128)(2,1)}), bf16[4,512,768]{2,1,0:T(8,128)(2,1)S(1)}, u32[]{:S(2)}, u32[]{:S(2)}) async-start(bf16[4,512,768]{2,1,0:T(8,128)(2,1)} %broadcast_in_dim.40), calls=%async_computation.3 | async-start | bytes 6291456 | tf_op jit(solution)/shard_map/all_to_all | solution.py:170
  281.4 25.4 %reduce-scatter.2.cloned.1.call-done = bf16[128,2048]{1,0:T(8,128)(2,1)} async-done(((bf16[4096,2048]{1,0:T(8,128)(2,1)}), bf16[128,2048]{1,0:T(8,128)(2,1)}) %reduce-scatter.2.cloned.1.call-update) | async-done | bytes 524304 | tf_op jit(solution)/shard_map/reduce_scatter | solution.py:136
  306.8 3.4 subtract_convert_fusion.1
  310.2 6.5 %all-to-all-done.2 = bf16[4,512,768]{2,1,0:T(8,128)(2,1)S(1)} async-done(((bf16[4,512,768]{2,1,0:T(8,128)(2,1)}), bf16[4,512,768]{2,1,0:T(8,128)(2,1)S(1)}, u32[]{:S(2)}, u32[]{:S(2)}) %all-to-all-start.2) | async-done | bytes 3145760 | tf_op jit(solution)/shard_map/all_to_all | solution.py:170
  316.7 20.5 %all-gather.6.cloned.1.call-done = bf16[1,384,2048]{2,1,0:T(8,128)(2,1)} async-done(((bf16[1,384,512]{2,1,0:T(8,128)(2,1)}), bf16[1,384,2048]{2,1,0:T(8,128)(2,1)}) %all-gather.6.cloned.1.call-update) | async-done | bytes 1572880 | tf_op jit(solution)/shard_map/all_gather | solution.py:173
  (69 shorter events, 25.8 us)
Async XLA Ops:
  7.2 103.3 %copy-start.14 = (bf16[128,2048]{1,0:T(8,128)(2,1)S(1)}, bf16[128,2048]{1,0:T(8,128)(2,1)}, u32[]{:S(2)}) copy-start(bf16[128,2048]{1,0:T(8,128)(2,1)} %param.11) | copy-start | bytes 1572868
  7.2 103.3 %all-gather.8.cloned.1.call-start = ((), (), s32[]{:S(2)}) async-start(), calls=%async_computation.6 | async-start | bytes 27033600 | tf_op jit(solution)/shard_map/all_gather | solution.py:91
  11.8 154.5 %all-gather.10.cloned.1.call-start = ((), (), s32[]{:S(2)}) async-start(), calls=%async_computation.7 | async-start | bytes 8650752 | tf_op jit(solution)/shard_map/all_gather | solution.py:95
  111.2 195.6 %reduce-scatter.2.cloned.1.call-start = ((), (), s32[]{:S(2)}) async-start(), calls=%async_computation.4 | async-start | bytes 17301504 | tf_op jit(solution)/shard_map/reduce_scatter | solution.py:136
  132.8 9.4 %copy-start.15 = (bf16[1,2048,768]{2,1,0:T(8,128)(2,1)S(1)}, bf16[1,2048,768]{2,1,0:T(8,128)(2,1)}, u32[]{:S(2)}) copy-start(bf16[1,2048,768]{2,1,0:T(8,128)(2,1)} %param.14) | copy-start | bytes 9437188
  152.8 3.2 copy-start.18
  152.9 3.2 copy-start.20
  156.8 3.6 %copy-start.16 = (f32[32,72]{1,0:T(8,128)}, f32[32,72]{1,0:T(8,128)S(1)}, u32[]{:S(2)}) copy-start(f32[32,72]{1,0:T(8,128)S(1)} %select_reduce_fusion) | copy-start | bytes 27652
  156.8 5.8 %copy-start.12 = (bf16[1,384,2048]{2,1,0:T(8,128)(2,1)S(1)}, bf16[1,384,2048]{2,1,0:T(8,128)(2,1)}, u32[]{:S(2)}) copy-start(bf16[1,384,2048]{2,1,0:T(8,128)(2,1)} %param.15) | copy-start | bytes 4718596
  160.3 2.2 copy-start.7
  166.3 5.0 %copy-start.1 = (f32[2304,384]{0,1:T(8,128)S(1)}, f32[2304,384]{0,1:T(8,128)}, u32[]{:S(2)}) copy-start(f32[2304,384]{0,1:T(8,128)} %get-tuple-element.16) | copy-start | bytes 10616836
  166.3 5.5 %copy-start.2 = (f32[2304,384]{0,1:T(8,128)S(1)}, f32[2304,384]{0,1:T(8,128)}, u32[]{:S(2)}) copy-start(f32[2304,384]{0,1:T(8,128)} %fusion.24) | copy-start | bytes 10616836
  166.3 5.9 %copy-start.13 = (bf16[1,384,2048]{2,1,0:T(8,128)(2,1)S(1)}, bf16[1,384,2048]{2,1,0:T(8,128)(2,1)}, u32[]{:S(2)}) copy-start(bf16[1,384,2048]{2,1,0:T(8,128)(2,1)} %param.15) | copy-start | bytes 4718596
  171.3 3.4 copy-start
  174.6 11.2 %copy-start.4 = (bf16[2304,384]{0,1:T(8,128)(2,1)}, bf16[2304,384]{0,1:T(8,128)(2,1)S(1)}, u32[]{:S(2)}) copy-start(bf16[2304,384]{0,1:T(8,128)(2,1)S(1)} %get-tuple-element.32) | copy-start | bytes 5308420
  174.6 11.2 %copy-start.6 = (bf16[2304,384]{0,1:T(8,128)(2,1)}, bf16[2304,384]{0,1:T(8,128)(2,1)S(1)}, u32[]{:S(2)}) copy-start(bf16[2304,384]{0,1:T(8,128)(2,1)S(1)} %get-tuple-element.33) | copy-start | bytes 5308420
  174.7 11.2 %copy-start.19 = (pred[32,128]{1,0:T(8,128)(4,1)S(1)}, pred[32,128]{1,0:T(8,128)(4,1)}, u32[]{:S(2)}) copy-start(pred[32,128]{1,0:T(8,128)(4,1)} %copy-done.17) | copy-start | bytes 12292
  203.2 5.2 %copy-start.5 = (bf16[2304,384]{0,1:T(8,128)(2,1)S(1)}, bf16[2304,384]{0,1:T(8,128)(2,1)}, u32[]{:S(2)}) copy-start(bf16[2304,384]{0,1:T(8,128)(2,1)} %copy-done.4) | copy-start | bytes 5308420
  204.5 24.2 %all-to-all-start = ((bf16[384,4,512]{2,0,1:T(8,128)(2,1)}), bf16[384,4,512]{2,0,1:T(8,128)(2,1)S(1)}, u32[]{:S(2)}, u32[]{:S(2)}) async-start(bf16[384,4,512]{2,0,1:T(8,128)(2,1)} %bitcast.36), calls=%async_computation.1 | async-start | bytes 3145728 | tf_op jit(solution)/shard_map/all_to_all | solution.py:153
  229.8 40.1 %all-to-all-start.1 = ((bf16[4,512,768]{2,1,0:T(8,128)(2,1)}), bf16[4,512,768]{2,1,0:T(8,128)(2,1)S(1)}, u32[]{:S(2)}, u32[]{:S(2)}) async-start(bf16[4,512,768]{2,1,0:T(8,128)(2,1)} %bitcast.49), calls=%async_computation.2 | async-start | bytes 6291456 | tf_op jit(solution)/shard_map/all_to_all | solution.py:146
  269.9 2.0 copy-start.10
  277.6 39.1 %all-to-all-start.2 = ((bf16[4,512,768]{2,1,0:T(8,128)(2,1)}), bf16[4,512,768]{2,1,0:T(8,128)(2,1)S(1)}, u32[]{:S(2)}, u32[]{:S(2)}) async-start(bf16[4,512,768]{2,1,0:T(8,128)(2,1)} %broadcast_in_dim.40), calls=%async_computation.3 | async-start | bytes 6291456 | tf_op jit(solution)/shard_map/all_to_all | solution.py:170
  281.3 55.9 %all-gather.6.cloned.1.call-start = ((), (), s32[]{:S(2)}) async-start(), calls=%async_computation.5 | async-start | bytes 1966080 | tf_op jit(solution)/shard_map/all_gather | solution.py:173
  337.2 2.5 copy-start.11
  (4 other events, 4.7 us)
Sparse Core Ops, SparseCore 0:
  11.9 98.4 all-gather.7
  113.3 52.3 all-gather.9
  194.2 112.5 reduce-scatter.1
  310.4 26.8 all-gather.5
where the time goes:
time: 348 us; the launch traced here: 347 us
  waiting for transfers between devices  193 us (55%)
  matrix products  77.2 us (22%)
  other arithmetic  26.3 us (8%)
  local copies, waits for them, and re-layouts  25.9 us (7%)
  between operations  14 us (4%)
  starting transfers between devices  11.5 us (3%)
    all_gather x1, waiting for transfers between devices, local(): lax.all_gather(jnp.concatenate([tokens, cotangent[:, :half_width], meta],...  98.6 us
    all_to_all x1, waiting for transfers between devices, local(): lax.all_to_all(grad_pair.astype(jnp.bfloat16).reshape(groups, share_rows,...  33.5 us
    reduce_scatter x1, waiting for transfers between devices, local(): lax.psum_scatter(dense.reshape(expert_count * local_tokens, model_width),...  25.4 us
    all_gather x1, waiting for transfers between devices, local(): full_down = lax.all_gather(new_down, 'group', axis=2, tiled=True)  20.5 us
    dot_general x1, matrix products, local(): jnp.einsum('srt,stc->src', pick_b, first, preferred_element_type=jnp.floa...  15.9 us
    dot_general x1, matrix products, expert_backward(): jnp.dot(inputs.T, pair_grad, preferred_element_type=jnp.float32)  12.5 us
    unnamed x45, local copies, waits for them, and re-layouts  11.6 us
    dot_general x1, matrix products, expert_backward(): jnp.dot(pair_grad, weight_gate_up.T, preferred_element_type=jnp.float32)  11.2 us
  transfers between devices with their start and end apart: 7, of which 6 were waited for; matrix products, arithmetic and copies ran while one was open for 25% of the time, Pallas kernels for 0%

commit v1 on v0

--- a/solution.py
+++ b/solution.py
@@ -170,7 +170,8 @@
     full_pair = lax.all_to_all(
         jnp.broadcast_to(new_pair, (groups, share_rows, pair_width)), "group", 0, 0, tiled=True
     ).reshape(1, model_width, pair_width)
-    full_down = lax.all_gather(new_down, "group", axis=2, tiled=True)
+    outgoing = jnp.stack([new_down] * lax.axis_size("group"))
+    full_down = jnp.concatenate(lax.all_to_all(outgoing, "group", 0, 0), axis=2)
     return (token_grad, full_pair, full_down, first_pair, second_pair, first_down, second_down)
 
 

time: 348 us -> 353 us (1.014)
  waiting for transfers between devices: 193 us -> 186 us
  starting transfers between devices: 11.5 us -> 16.4 us
  local copies, waits for them, and re-layouts: 25.9 us -> 29.7 us
    all_gather x1 -> x0, waiting for transfers between devices: 20.5 us -> none  [local(): full_down = lax.all_gather(new_down, 'group', axis=2, tiled=True)]
    all_to_all x0 -> x1, waiting for transfers between devices: none -> 17.7 us  [local(): full_down = jnp.concatenate(lax.all_to_all(outgoing, 'group', 0, 0), axis=2)]
    all_to_all x1, waiting for transfers between devices: 33.5 us -> 26.8 us  [local(): lax.all_to_all(grad_pair.astype(jnp.bfloat16).reshape(groups, share_rows,...]
    all_to_all x1, waiting for transfers between devices: 7.91 us -> 13.7 us  [local(): lax.all_to_all(grad_down.astype(jnp.bfloat16).reshape(hidden_count, group...]
    all_to_all x0 -> x1, starting transfers between devices: none -> 4.35 us  [local(): full_down = jnp.concatenate(lax.all_to_all(outgoing, 'group', 0, 0), axis=2)]
    unnamed x45 -> x41, local copies, waits for them, and re-layouts: 11.6 us -> 11.5 us
where the time goes in v1:
time: 353 us; the launch traced here: 350 us
  waiting for transfers between devices  186 us (53%)
  matrix products  77.5 us (22%)
  local copies, waits for them, and re-layouts  29.7 us (8%)
  other arithmetic  26.1 us (7%)
  starting transfers between devices  16.4 us (5%)
  between operations  14 us (4%)
    all_gather x1, waiting for transfers between devices, local(): lax.all_gather(jnp.concatenate([tokens, cotangent[:, :half_width], meta],...  98.6 us
    all_to_all x1, waiting for transfers between devices, local(): lax.all_to_all(grad_pair.astype(jnp.bfloat16).reshape(groups, share_rows,...  26.8 us
    reduce_scatter x1, waiting for transfers between devices, local(): lax.psum_scatter(dense.reshape(expert_count * local_tokens, model_width),...  26.2 us
    all_to_all x1, waiting for transfers between devices, local(): full_down = jnp.concatenate(lax.all_to_all(outgoing, 'group', 0, 0), axis=2)  17.7 us
    dot_general x1, matrix products, local(): jnp.einsum('srt,stc->src', pick_b, first, preferred_element_type=jnp.floa...  15.9 us
    all_to_all x1, waiting for transfers between devices, local(): lax.all_to_all(grad_down.astype(jnp.bfloat16).reshape(hidden_count, group...  13.7 us
    unnamed x41, local copies, waits for them, and re-layouts  11.5 us
    dot_general x1, matrix products, expert_backward(): jnp.dot(inputs.T, pair_grad, preferred_element_type=jnp.float32)  11.2 us
  transfers between devices with their start and end apart: 7, of which 6 were waited for; matrix products, arithmetic and copies ran while one was open for 25% of the time, Pallas kernels for 0%

profile of v1, /device:TPU:1, one launch (start us, length us, event | category | flops | bytes accessed | tf_op | source)
XLA Modules:
  0.0 350.0 jit_solution(2214300360844579427)
XLA Ops:
  11.8 98.6 %all-gather.5.cloned.1.call-done = bf16[4096,3200]{1,0:T(8,128)(2,1)} async-done(((bf16[128,3200]{1,0:T(8,128)(2,1)}), bf16[4096,3200]{1,0:T(8,128)(2,1)}) %all-gather.5.cloned.1.call-update) | async-done | bytes 26214416 | tf_op jit(solution)/shard_map/all_gather | solution.py:91
  112.7 3.0 fusion.12
  116.9 15.9 %convolution_convert_fusion.1 = bf16[32,72,3200]{2,1,0:T(8,128)(2,1)} fusion(bf16[32,128,3200]{2,1,0:T(8,128)(2,1)} %bitcast.46, f32[32,128]{1,0:T(8,128)S(1)} %fusion.34, pred[32,128]{1,0:T(8,128)(4,1)S(1)} %convert_compare_fusion), kind=kOutput, calls=%fused_computation.1 | convolution fusion | flops 1895399424 | bytes 40980480 | tf_op jit(solution)/shard_map/srt,stc->src/dot_general | solution.py:111
  132.8 9.4 %slice.59 = bf16[32,72,2048]{2,1,0:T(8,128)(2,1)} slice(bf16[32,72,3200]{2,1,0:T(8,128)(2,1)} %convolution_convert_fusion.1), slice={[0:32], [0:72], [0:2048]} | slice | bytes 18874368 | tf_op jit(solution)/shard_map/slice | solution.py:114
  142.3 10.6 %fusion.6 = f32[2304,768]{0,1:T(8,128)S(1)} fusion(bf16[2304,2048]{1,0:T(8,128)(2,1)} %bitcast.49, bf16[1,2048,768]{2,1,0:T(8,128)(2,1)S(1)} %copy-done.13), kind=kOutput, calls=%fused_computation.20 | convolution fusion | flops 7247757312 | bytes 19660800 | tf_op jit(solution)/shard_map/dot_general | solution.py:15
  152.9 3.2 fusion.4
  156.8 3.5 %multiply_convert_fusion.1 = bf16[32,72,1024]{2,1,0:T(8,128)(2,1)S(1)} fusion(bf16[32,72,3200]{2,1,0:T(8,128)(2,1)} %convolution_convert_fusion.1, f32[32,72]{1,0:T(8,128)S(1)} %select_reduce_fusion), kind=kLoop, calls=%fused_computation.8 | loop fusion | flops 7077888 | bytes 9446400 | tf_op jit(solution)/shard_map/convert_element_type | solution.py:121
  162.6 3.8 %fusion.24 = f32[2304,384]{0,1:T(8,128)} fusion(bf16[2304,1024]{1,0:T(8,128)(2,1)S(1)} %bitcast.54, bf16[384,2048]{1,0:T(8,128)(2,1)S(1)} %bitcast.59), kind=kOutput, calls=%fused_computation.46 | convolution fusion | flops 1811939328 | bytes 9043968 | tf_op jit(solution)/shard_map/dot_general | solution.py:23
  166.3 4.9 %multiply_convert_fusion = bf16[32,72,1024]{2,1,0:T(8,128)(2,1)S(1)} fusion(f32[32,72]{1,0:T(8,128)} %copy-done.14, bf16[32,128,1024]{2,1,0:T(8,128)(2,1)} %bitcast.51, f32[32,128]{1,0:T(8,128)S(1)} %fusion.34, pred[32,128]{1,0:T(8,128)(4,1)} %copy-done.15), kind=kOutput, calls=%fused_computation.7 | convolution fusion | flops 614006784 | bytes 13136896 | tf_op jit(solution)/shard_map/srt,stc->src/dot_general | solution.py:116
  174.7 11.2 %convolution_convert_fusion.2 = bf16[2304,2048]{1,0:T(8,128)(2,1)S(1)} fusion(bf16[1,2048,768]{2,1,0:T(8,128)(2,1)} %param.14, bf16[2304,384]{0,1:T(8,128)(2,1)S(1)} %get-tuple-element.40, bf16[2304,384]{0,1:T(8,128)(2,1)S(1)} %get-tuple-element.39), kind=kOutput, calls=%fused_computation.2 | convolution fusion | flops 7259553792 | bytes 16121856 | tf_op jit(solution)/shard_map/dot_general | solution.py:42
  185.9 8.2 %convolution_convert_fusion = bf16[32,128,2048]{2,1,0:T(8,128)(2,1)} fusion(bf16[32,72,2048]{2,1,0:T(8,128)(2,1)S(1)} %bitcast.47, f32[32,128]{1,0:T(8,128)S(1)} %fusion.34, pred[32,128]{1,0:T(8,128)(4,1)S(1)} %copy-done.17), kind=kOutput, calls=%fused_computation | convolution fusion | flops 1216937984 | bytes 26234880 | tf_op jit(solution)/shard_map/srt,src->stc/dot_general | solution.py:130
  196.1 11.2 %convolution_convert_fusion.3 = bf16[2048,768]{1,0:T(8,128)(2,1)} fusion(bf16[2304,2048]{1,0:T(8,128)(2,1)} %bitcast.50, bf16[2304,384]{0,1:T(8,128)(2,1)S(1)} %copy-done.6, bf16[2304,384]{0,1:T(8,128)(2,1)S(1)} %copy-done.4), kind=kOutput, calls=%fused_computation.18 | convolution fusion | flops 7256408064 | bytes 16121856 | tf_op jit(solution)/shard_map/dot_general | solution.py:41
  207.4 3.9 %all-to-all-start.1 = ((bf16[4,512,768]{2,1,0:T(8,128)(2,1)}), bf16[4,512,768]{2,1,0:T(8,128)(2,1)S(1)}, u32[]{:S(2)}, u32[]{:S(2)}) async-start(bf16[4,512,768]{2,1,0:T(8,128)(2,1)} %bitcast.56), calls=%async_computation.2 | async-start | bytes 6291456 | tf_op jit(solution)/shard_map/all_to_all | solution.py:146
  211.2 9.1 %fusion.8 = bf16[384,2048]{1,0:T(8,128)(2,1)S(1)} fusion(bf16[2304,384]{0,1:T(8,128)(2,1)} %get-tuple-element.18, bf16[2304,1024]{1,0:T(8,128)(2,1)} %bitcast.44, bf16[2304,1024]{1,0:T(8,128)(2,1)} %bitcast.55), kind=kOutput, calls=%fused_computation.23 | convolution fusion | flops 3643539456 | bytes 12779520 | tf_op jit(solution)/shard_map/dot_general | solution.py:38
  221.7 26.8 %all-to-all-done.1 = bf16[4,512,768]{2,1,0:T(8,128)(2,1)S(1)} async-done(((bf16[4,512,768]{2,1,0:T(8,128)(2,1)}), bf16[4,512,768]{2,1,0:T(8,128)(2,1)S(1)}, u32[]{:S(2)}, u32[]{:S(2)}) %all-to-all-start.1) | async-done | bytes 3145760 | tf_op jit(solution)/shard_map/all_to_all | solution.py:146
  248.5 4.4 %all-to-all-start = ((bf16[384,4,512]{2,0,1:T(8,128)(2,1)}), bf16[384,4,512]{2,0,1:T(8,128)(2,1)}, u32[]{:S(2)}, u32[]{:S(2)}) async-start(bf16[384,4,512]{2,0,1:T(8,128)(2,1)} %bitcast.52), calls=%async_computation.1 | async-start | bytes 3145728 | tf_op jit(solution)/shard_map/all_to_all | solution.py:153
  254.8 3.9 %fusion.26 = (bf16[512,768]{1,0:T(8,128)(2,1)S(1)}, f32[1,512,768]{2,1,0:T(8,128)}, f32[1,512,768]{2,1,0:T(8,128)}) fusion(bf16[1,2048,768]{2,1,0:T(8,128)(2,1)} %param.14, s32[]{:T(128)S(6)} %select_n.14, f32[512,768]{1,0:T(8,128)S(1)} %convert_reduce_fusion, f32[1,512,768]{2,1,0:T(8,128)S(1)} %copy-done.8, f32[1,512,768]{2,1,0:T(8,128)S(1)} %copy-done.9), kind=kLoop, calls=%fused_computation.50 | loop fusion | flops 5111808 | bytes 9437188 | tf_op jit(solution)/shard_map/broadcast_in_dim | solution.py:171
  258.7 13.7 %all-to-all-done = bf16[384,4,512]{2,0,1:T(8,128)(2,1)} async-done(((bf16[384,4,512]{2,0,1:T(8,128)(2,1)}), bf16[384,4,512]{2,0,1:T(8,128)(2,1)}, u32[]{:S(2)}, u32[]{:S(2)}) %all-to-all-start) | async-done | bytes 1572896 | tf_op jit(solution)/shard_map/all_to_all | solution.py:153
  274.2 3.7 %all-to-all-start.2 = ((bf16[4,512,768]{2,1,0:T(8,128)(2,1)}), bf16[4,512,768]{2,1,0:T(8,128)(2,1)S(1)}, u32[]{:S(2)}, u32[]{:S(2)}) async-start(bf16[4,512,768]{2,1,0:T(8,128)(2,1)} %broadcast_in_dim.40), calls=%async_computation.3 | async-start | bytes 6291456 | tf_op jit(solution)/shard_map/all_to_all | solution.py:170
  280.6 26.2 %reduce-scatter.2.cloned.1.call-done = bf16[128,2048]{1,0:T(8,128)(2,1)} async-done(((bf16[4096,2048]{1,0:T(8,128)(2,1)}), bf16[128,2048]{1,0:T(8,128)(2,1)}) %reduce-scatter.2.cloned.1.call-update) | async-done | bytes 524304 | tf_op jit(solution)/shard_map/reduce_scatter | solution.py:136
  306.8 3.4 fusion.33
  310.2 3.2 all-to-all-done.2
  314.6 4.3 %all-to-all-start.3 = ((bf16[4,1,384,512]{3,2,1,0:T(8,128)(2,1)}), bf16[4,1,384,512]{3,2,1,0:T(8,128)(2,1)}, u32[]{:S(2)}, u32[]{:S(2)}) async-start(bf16[4,1,384,512]{3,2,1,0:T(8,128)(2,1)} %stack.2), calls=%async_computation.4 | async-start | bytes 3145728 | tf_op jit(solution)/shard_map/all_to_all | solution.py:174
  319.0 17.7 %all-to-all-done.3 = bf16[4,1,384,512]{3,2,1,0:T(8,128)(2,1)} async-done(((bf16[4,1,384,512]{3,2,1,0:T(8,128)(2,1)}), bf16[4,1,384,512]{3,2,1,0:T(8,128)(2,1)}, u32[]{:S(2)}, u32[]{:S(2)}) %all-to-all-start.3) | async-done | bytes 1572896 | tf_op jit(solution)/shard_map/all_to_all | solution.py:174
  (66 shorter events, 32.1 us)
Async XLA Ops:
  7.2 103.3 %copy-start.12 = (bf16[128,2048]{1,0:T(8,128)(2,1)S(1)}, bf16[128,2048]{1,0:T(8,128)(2,1)}, u32[]{:S(2)}) copy-start(bf16[128,2048]{1,0:T(8,128)(2,1)} %param.11) | copy-start | bytes 1572868
  7.2 103.3 %all-gather.5.cloned.1.call-start = ((), (), s32[]{:S(2)}) async-start(), calls=%async_computation.6 | async-start | bytes 27033600 | tf_op jit(solution)/shard_map/all_gather | solution.py:91
  11.8 154.6 %all-gather.7.cloned.1.call-start = ((), (), s32[]{:S(2)}) async-start(), calls=%async_computation.7 | async-start | bytes 8650752 | tf_op jit(solution)/shard_map/all_gather | solution.py:95
  111.2 195.6 %reduce-scatter.2.cloned.1.call-start = ((), (), s32[]{:S(2)}) async-start(), calls=%async_computation.5 | async-start | bytes 17301504 | tf_op jit(solution)/shard_map/reduce_scatter | solution.py:136
  132.8 9.4 %copy-start.13 = (bf16[1,2048,768]{2,1,0:T(8,128)(2,1)S(1)}, bf16[1,2048,768]{2,1,0:T(8,128)(2,1)}, u32[]{:S(2)}) copy-start(bf16[1,2048,768]{2,1,0:T(8,128)(2,1)} %param.14) | copy-start | bytes 9437188
  152.9 3.3 copy-start.16
  152.9 3.2 copy-start.18
  156.8 3.5 %copy-start.14 = (f32[32,72]{1,0:T(8,128)}, f32[32,72]{1,0:T(8,128)S(1)}, u32[]{:S(2)}) copy-start(f32[32,72]{1,0:T(8,128)S(1)} %select_reduce_fusion) | copy-start | bytes 27652
  156.8 5.8 %copy-start.10 = (bf16[1,384,2048]{2,1,0:T(8,128)(2,1)S(1)}, bf16[1,384,2048]{2,1,0:T(8,128)(2,1)}, u32[]{:S(2)}) copy-start(bf16[1,384,2048]{2,1,0:T(8,128)(2,1)} %param.15) | copy-start | bytes 4718596
  160.3 2.2 copy-start.7
  166.3 5.0 %copy-start.1 = (f32[2304,384]{0,1:T(8,128)S(1)}, f32[2304,384]{0,1:T(8,128)}, u32[]{:S(2)}) copy-start(f32[2304,384]{0,1:T(8,128)} %get-tuple-element.16) | copy-start | bytes 10616836
  166.3 5.5 %copy-start.2 = (f32[2304,384]{0,1:T(8,128)S(1)}, f32[2304,384]{0,1:T(8,128)}, u32[]{:S(2)}) copy-start(f32[2304,384]{0,1:T(8,128)} %fusion.24) | copy-start | bytes 10616836
  166.3 5.9 %copy-start.11 = (bf16[1,384,2048]{2,1,0:T(8,128)(2,1)S(1)}, bf16[1,384,2048]{2,1,0:T(8,128)(2,1)}, u32[]{:S(2)}) copy-start(bf16[1,384,2048]{2,1,0:T(8,128)(2,1)} %param.15) | copy-start | bytes 4718596
  171.3 3.4 copy-start
  174.7 11.2 %copy-start.3 = (bf16[2304,384]{0,1:T(8,128)(2,1)}, bf16[2304,384]{0,1:T(8,128)(2,1)S(1)}, u32[]{:S(2)}) copy-start(bf16[2304,384]{0,1:T(8,128)(2,1)S(1)} %get-tuple-element.39) | copy-start | bytes 5308420
  174.7 11.2 %copy-start.5 = (bf16[2304,384]{0,1:T(8,128)(2,1)}, bf16[2304,384]{0,1:T(8,128)(2,1)S(1)}, u32[]{:S(2)}) copy-start(bf16[2304,384]{0,1:T(8,128)(2,1)S(1)} %get-tuple-element.40) | copy-start | bytes 5308420
  174.7 11.2 %copy-start.17 = (pred[32,128]{1,0:T(8,128)(4,1)S(1)}, pred[32,128]{1,0:T(8,128)(4,1)}, u32[]{:S(2)}) copy-start(pred[32,128]{1,0:T(8,128)(4,1)} %copy-done.15) | copy-start | bytes 12292
  194.1 1.5 copy-start.4
  194.1 2.0 copy-start.6
  207.4 41.1 %all-to-all-start.1 = ((bf16[4,512,768]{2,1,0:T(8,128)(2,1)}), bf16[4,512,768]{2,1,0:T(8,128)(2,1)S(1)}, u32[]{:S(2)}, u32[]{:S(2)}) async-start(bf16[4,512,768]{2,1,0:T(8,128)(2,1)} %bitcast.56), calls=%async_computation.2 | async-start | bytes 6291456 | tf_op jit(solution)/shard_map/all_to_all | solution.py:146
  248.5 23.9 %all-to-all-start = ((bf16[384,4,512]{2,0,1:T(8,128)(2,1)}), bf16[384,4,512]{2,0,1:T(8,128)(2,1)}, u32[]{:S(2)}, u32[]{:S(2)}) async-start(bf16[384,4,512]{2,0,1:T(8,128)(2,1)} %bitcast.52), calls=%async_computation.1 | async-start | bytes 3145728 | tf_op jit(solution)/shard_map/all_to_all | solution.py:153
  252.9 1.9 copy-start.9
  274.2 39.1 %all-to-all-start.2 = ((bf16[4,512,768]{2,1,0:T(8,128)(2,1)}), bf16[4,512,768]{2,1,0:T(8,128)(2,1)S(1)}, u32[]{:S(2)}, u32[]{:S(2)}) async-start(bf16[4,512,768]{2,1,0:T(8,128)(2,1)} %broadcast_in_dim.40), calls=%async_computation.3 | async-start | bytes 6291456 | tf_op jit(solution)/shard_map/all_to_all | solution.py:170
  314.6 22.1 %all-to-all-start.3 = ((bf16[4,1,384,512]{3,2,1,0:T(8,128)(2,1)}), bf16[4,1,384,512]{3,2,1,0:T(8,128)(2,1)}, u32[]{:S(2)}, u32[]{:S(2)}) async-start(bf16[4,1,384,512]{3,2,1,0:T(8,128)(2,1)} %stack.2), calls=%async_computation.4 | async-start | bytes 3145728 | tf_op jit(solution)/shard_map/all_to_all | solution.py:174
  (2 other events, 2.0 us)
Sparse Core Ops, SparseCore 0:
  11.9 98.4 all-gather.4
  113.3 52.3 all-gather.6
  194.3 112.4 reduce-scatter.1
